TPU v7x, 128 devices: a whole 4x4x4 slice. The times are simulated.
128 devices in a mesh: blk: 32 (over x, z, y_hi), sub: 4 (over y_lo, core).
Axes of the slice: x: 4, y: 4 (y_hi: 2, y_lo: 2; y = y_hi * 2 + y_lo), z: 4, core: 2. Of those that a mesh axis runs over, the one named last changes fastest.
Arguments:
- phase: float32 [6, 131072], P(None, ('blk', 'sub')), may hold values from -6 to 6
- derivs: float32 [6, 131072], P(None, ('blk', 'sub')), may hold values from -6 to 6
- mass: float32 [131072], P(('blk', 'sub')), may hold values from 1.5258789e-05 to 0.00024414062
- elapsed: float32 [131072], P(('blk', 'sub')), may hold values from 0.05 to 0.5
- active_slots: int32 [3, 8192], P(None, ('blk', 'sub')), may hold values from 0 to 1023, as said below
- active_counts: int32 [3, 128], P(None, ('blk', 'sub')), may hold values from 33 to 64, as said below
Outputs:
- new_phase: float32 [6, 131072], P(None, ('blk', 'sub'))
- new_derivs: float32 [6, 131072], P(None, ('blk', 'sub'))
- active_forces: float32 [6, 3, 8192], P(None, None, ('blk', 'sub'))
Inputs may be any that keep to these rules, and one draw needn't show every extreme that they name: `active_slots`: on each device the 192 entries, padding included, are distinct slots of that device's own stars. `active_counts`: in every level some device's list is full.
All inputs are finite; a program needn't handle non-finite values.
Results may differ from a plain program's by a relative error of at most 0.00027.
Values sent between devices are 32-bit elements; how exact they have to be, the bound alone decides.
No kernel may reach another device: no remote copies, remote signals or barrier semaphores. Data moves between devices by JAX's collectives and lax.ppermute only.
A program may use at most 64 MiB of HBM per device.

v0:
```python
import jax
import jax.numpy as jnp
from jax import lax
from jax.experimental import pallas as pl
from jax.experimental.pallas import tpu as pltpu
from jax.sharding import PartitionSpec as P

LEVELS = 3
LCAP = 64
SUBLANES = 8
LANES = 128

SOFTEN_SQ = 0.0025
N_CHUNKS = 2


def predict(phase, derivs, elapsed):
    t_now = elapsed[None, :]
    pos_pred = (
        phase[:3]
        + t_now * phase[3:]
        + t_now * t_now / 2.0 * derivs[:3]
        + t_now * t_now * t_now / 6.0 * derivs[3:]
    )
    vel_pred = phase[3:] + t_now * derivs[:3] + t_now * t_now / 2.0 * derivs[3:]
    return (pos_pred, vel_pred)


def correct(pred_rows, old_rows, step_len, new_forces):
    diff_acc = old_rows[:3] - new_forces[:3]
    step_row = step_len[None, :]
    term_two = -6.0 * diff_acc - step_row * (4.0 * old_rows[3:] + 2.0 * new_forces[3:])
    term_three = 12.0 * diff_acc + 6.0 * step_row * (old_rows[3:] + new_forces[3:])
    pos_new = pred_rows[:3] + step_row * step_row * (term_two / 24.0 + term_three / 120.0)
    vel_new = pred_rows[3:] + step_row * (term_two / 6.0 + term_three / 24.0)
    return jnp.concatenate([pos_new, vel_new], axis=0)


def pair_sums(row, stars, accs):
    xi, yi, zi, ui, vi, wi = row
    xk, yk, zk, uk, vk, wk, mk = stars
    dx = xk - xi
    dy = yk - yi
    dz = zk - zi
    du = uk - ui
    dv = vk - vi
    dw = wk - wi
    dist_sq = dx * dx + dy * dy + dz * dz + SOFTEN_SQ
    inverse = lax.rsqrt(dist_sq)
    inv_sq = inverse * inverse
    weight = mk * (inv_sq * inverse)
    radial = (weight * inv_sq) * (dx * du + dy * dv + dz * dw)
    ax, ay, az, jx, jy, jz, qx, qy, qz = accs
    return (
        ax + weight * dx,
        ay + weight * dy,
        az + weight * dz,
        jx + weight * du,
        jy + weight * dv,
        jz + weight * dw,
        qx + radial * dx,
        qy + radial * dy,
        qz + radial * dz,
    )


def forces_kernel(pairs_ref, rows_ref, stars_ref, acc_ref, out_ref):
    n_rows = out_ref.shape[1]
    n_blocks = pairs_ref.shape[0]
    per_block = n_rows // n_blocks
    n_vregs = stars_ref.shape[1] // SUBLANES
    zero = jnp.zeros((SUBLANES, LANES), jnp.float32)
    out_ref[...] = acc_ref[...]

    def row_scalars(r):
        return tuple(rows_ref[c * n_rows + r] for c in range(6))

    for block in range(n_blocks):

        def pair_body(p, carry, block=block):
            r0 = block * per_block + 2 * p
            r1 = r0 + 1
            row0 = row_scalars(r0)
            row1 = row_scalars(r1)

            def star_body(j, accs):
                base = pl.multiple_of(j * SUBLANES, SUBLANES)
                stars = tuple(stars_ref[c, pl.ds(base, SUBLANES), :] for c in range(7))
                return pair_sums(row0, stars, accs[:9]) + pair_sums(row1, stars, accs[9:])

            accs = lax.fori_loop(0, n_vregs, star_body, (zero,) * 18, unroll=2)
            for r, part in ((r0, accs[:9]), (r1, accs[9:])):
                ax, ay, az, jx, jy, jz, qx, qy, qz = part
                vals = (ax, ay, az, jx - 3.0 * qx, jy - 3.0 * qy, jz - 3.0 * qz)
                for c in range(6):
                    out_ref[c, pl.ds(r, 1), :] = out_ref[c, pl.ds(r, 1), :] + jnp.sum(
                        vals[c], axis=0, keepdims=True
                    )
            return carry

        lax.fori_loop(0, pairs_ref[block], pair_body, 0)


def add_forces(pairs, rows, stars, acc):
    n_rows = rows.shape[1]
    n_stars = stars.shape[1] * LANES
    return pl.pallas_call(
        forces_kernel,
        out_shape=jax.ShapeDtypeStruct(acc.shape, jnp.float32),
        in_specs=[
            pl.BlockSpec(memory_space=pltpu.SMEM),
            pl.BlockSpec(memory_space=pltpu.SMEM),
            pl.BlockSpec(memory_space=pltpu.VMEM),
            pl.BlockSpec(memory_space=pltpu.VMEM),
        ],
        out_specs=pl.BlockSpec(memory_space=pltpu.VMEM),
        input_output_aliases={3: 0},
        cost_estimate=pl.CostEstimate(
            flops=40 * n_rows * n_stars,
            transcendentals=n_rows * n_stars,
            bytes_accessed=4 * (stars.size + 2 * acc.size),
        ),
    )(pairs, rows.reshape(-1), stars, acc)


def on_device(phase, derivs, mass, elapsed, active_slots, active_counts):
    pred_pos, pred_vel = predict(phase, derivs, elapsed)
    slot_rows = active_slots.reshape(-1)
    live_grid = lax.broadcasted_iota(jnp.int32, (LEVELS, LCAP), 1) < active_counts
    is_live = live_grid.reshape(-1)
    targets = jnp.concatenate([pred_pos[:, slot_rows], pred_vel[:, slot_rows]], axis=0)

    n_sub = lax.axis_size("sub")
    me = lax.axis_index("sub")
    group_rows = lax.all_gather(targets, "sub", axis=1, tiled=True)
    group_counts = lax.all_gather(active_counts.reshape(-1), "sub", axis=0, tiled=True)
    n_blocks = group_counts.shape[0]
    per_block = LCAP // n_sub
    dealt = group_rows.reshape(6, n_blocks, per_block, n_sub)
    my_rows = lax.dynamic_slice_in_dim(dealt, me, 1, axis=3).reshape(6, n_blocks * per_block)
    my_counts = jnp.maximum(group_counts - me + n_sub - 1, 0) // n_sub
    my_pairs = (my_counts + 1) // 2

    n_local = phase.shape[1]
    local_stars = jnp.concatenate([pred_pos, pred_vel, mass[None, :]], axis=0)
    local_stars = local_stars.reshape(7, n_local // LANES, LANES)
    n_chunks = N_CHUNKS
    rows_per_chunk = local_stars.shape[1] // n_chunks
    acc = jnp.zeros((6, n_blocks * per_block, LANES), jnp.float32)
    for chunk in range(n_chunks):
        piece = local_stars[:, chunk * rows_per_chunk:(chunk + 1) * rows_per_chunk, :]
        stars = lax.all_gather(piece, ("blk", "sub"), axis=1, tiled=True)
        acc = add_forces(my_pairs, my_rows, stars, acc)
    my_forces = jnp.sum(acc, axis=2).reshape(6, n_blocks, per_block, 1)

    placed = jnp.where(
        lax.broadcasted_iota(jnp.int32, (1, 1, 1, n_sub), 3) == me, my_forces, 0.0
    ).reshape(6, n_blocks * LCAP)
    new_forces = lax.psum_scatter(placed, "sub", scatter_dimension=1, tiled=True)

    shaped_forces = new_forces.reshape(6, LEVELS, LCAP)
    active_forces = jnp.where(live_grid[None, :, :], shaped_forces, jnp.zeros_like(shaped_forces))
    corrected = correct(targets, derivs[:, slot_rows], elapsed[slot_rows], new_forces)
    kept_phase = jnp.where(is_live[None, :], corrected, phase[:, slot_rows])
    kept_derivs = jnp.where(is_live[None, :], new_forces, derivs[:, slot_rows])
    new_phase = phase.at[:, slot_rows].set(kept_phase)
    new_derivs = derivs.at[:, slot_rows].set(kept_derivs)
    return (new_phase, new_derivs, active_forces)


def solution(mesh):
    in_specs = (
        P(None, ("blk", "sub")),
        P(None, ("blk", "sub")),
        P(("blk", "sub")),
        P(("blk", "sub")),
        P(None, ("blk", "sub")),
        P(None, ("blk", "sub")),
    )
    out_specs = (P(None, ("blk", "sub")), P(None, ("blk", "sub")), P(None, None, ("blk", "sub")))
    return jax.shard_map(
        on_device, mesh=mesh, in_specs=in_specs, out_specs=out_specs, check_vma=False
    )
```

profile of v0, /device:TPU:1, one launch (start us, length us, event | category | flops | bytes accessed | tf_op | source)
XLA Modules:
  0.0 275.3 jit_solution(7898539513232670346)
XLA Ops:
  7.2 0.7 multiply_multiply_fusion.1
  7.9 0.9 multiply_add_fusion
  8.8 0.7 pad_maximum_fusion
  9.5 0.6 fusion.3
  10.2 0.7 all-gather.5.cloned.1.call-update
  11.0 1.2 dynamic-slice
  12.9 0.8 bitcast_dynamic-update-slice_fusion
  13.6 5.1 %all-reduce = s32[12]{0:T(128)S(1)} all-reduce(s32[12]{0:T(128)S(1)} %bitcast_dynamic-update-slice_fusion), channel_id=2, replica_groups=mesh['blk'=32,'sub'=4] {'sub'}, use_global_device_ids=true, to_apply=%add | all-reduce | flops 12 | bytes 96
  19.2 0.8 reshape.106
  20.0 1.2 gather_fusion.1
  21.2 0.7 gather_fusion.3
  21.9 0.7 gather_fusion
  22.7 6.4 %all-gather.1 = f32[4,192,6]{1,2,0:T(8,128)S(1)} all-gather(f32[1,192,6]{1,2,0:T(8,128)S(1)} %maximum_bitcast_fusion), channel_id=1, replica_groups=mesh['blk'=32,'sub'=4] {'sub'}, dimensions={0}, use_global_device_ids=true | all-gather | bytes 23040 | tf_op jit(solution)/shard_map/all_gather | solution.py:135
  30.3 0.7 reshape_reshape.4.rows_ref
  31.1 0.6 and_select_fusion.pairs_ref
  31.7 49.1 %all-gather.7.cloned.1.call-done = f32[7,512,128]{2,0,1:T(8,128)} async-done(((f32[7,4,128]{2,0,1:T(8,128)}), f32[7,512,128]{2,0,1:T(8,128)}) %all-gather.7.cloned.1.call-update) | async-done | bytes 1835024 | tf_op jit(solution)/shard_map/all_gather | solution.py:152
  80.8 3.2 %copy.190.stars_ref = f32[7,512,128]{2,1,0:T(8,128)} copy(f32[7,512,128]{2,0,1:T(8,128)} %all-gather.7.cloned.1.call-done) | data formatting | bytes 3670016 | tf_op jit(solution)/shard_map/all_gather | solution.py:152
  84.0 0.9 broadcast_in_dim.69.acc_ref
  84.9 69.9 %shard_map.85.acc_ref = f32[6,192,128]{2,1,0:T(8,128)} custom-call(s32[12]{0:T(128)} %and_select_fusion.pairs_ref, f32[1152]{0:T(1024)} %reshape_reshape.4.rows_ref, f32[7,512,128]{2,1,0:T(8,128)} %copy.190.stars_ref, f32[6,192,128]{2,1,0:T(8,128)} %broadcast_in_dim.69.acc_ref), custom_call_target="tpu_custom_call", output_to_operand_aliasing={{}: (3, {})} | custom-call | flops 503316480 | bytes 3014656 | tf_op jit(solution)/shard_map/pallas_call | solution.py:107
  154.8 3.2 %copy.191.stars_ref = f32[7,512,128]{2,1,0:T(8,128)} copy(f32[7,512,128]{2,0,1:T(8,128)} %all-gather.5.cloned.1.call-done) | data formatting | bytes 3670016 | tf_op jit(solution)/shard_map/all_gather | solution.py:152
  157.9 69.9 %shard_map.86 = f32[6,192,128]{2,1,0:T(8,128)} custom-call(s32[12]{0:T(128)} %and_select_fusion.pairs_ref, f32[1152]{0:T(1024)} %reshape_reshape.4.rows_ref, f32[7,512,128]{2,1,0:T(8,128)} %copy.191.stars_ref, f32[6,192,128]{2,1,0:T(8,128)} %shard_map.85.acc_ref), custom_call_target="tpu_custom_call", output_to_operand_aliasing={{}: (3, {})} | custom-call | flops 503316480 | bytes 3014656 | tf_op jit(solution)/shard_map/pallas_call | solution.py:107
  227.8 1.4 reduce_sum.9
  229.8 0.9 copy.200
  231.3 0.7 gather_fusion.2
  232.1 0.7 gather_fusion.4
  233.0 29.7 %reduce-scatter.4.cloned.1.call-done = f32[192,6]{1,0:T(8,128)} async-done(((f32[768,6]{1,0:T(8,128)}), f32[192,6]{1,0:T(8,128)}) %reduce-scatter.4.cloned.1.call-update) | async-done | bytes 4624
  262.7 1.0 copy.201
  263.9 1.2 scatter_fusion.1
  265.2 0.8 copy.199
  266.1 1.2 scatter_fusion
  267.3 0.8 copy.198
  268.1 0.6 broadcast_select_fusion.1
  (46 shorter events, 3.8 us)
Async XLA Ops:
  7.2 12.8 %copy-start = (f32[1024]{0:T(1024)S(1)}, f32[1024]{0:T(1024)}, u32[]{:S(2)}) copy-start(f32[1024]{0:T(1024)} %param.9) | copy-start | bytes 12292
  7.2 73.6 %all-gather.7.cloned.1.call-start = ((), (), s32[]{:S(2)}) async-start(), calls=%async_computation.2 | async-start | bytes 2113536 | tf_op jit(solution)/shard_map/all_gather | solution.py:152
  10.1 144.6 %all-gather.5.cloned.1.call-start = ((), (), s32[]{:S(2)}) async-start(), calls=%async_computation.1 | async-start | bytes 2113536 | tf_op jit(solution)/shard_map/all_gather | solution.py:152
  10.9 251.8 %reduce-scatter.4.cloned.1.call-start = ((), (), s32[]{:S(2)}) async-start(), calls=%async_computation.3 | async-start | bytes 491520
  227.8 3.0 %copy-start.3 = (s32[3,1]{0,1:T(1,128)S(1)}, s32[3,1]{0,1:T(1,128)}, u32[]{:S(2)}) copy-start(s32[3,1]{0,1:T(1,128)} %param.11) | copy-start | bytes 40
  227.8 3.1 %copy-start.1 = (f32[6,1024]{1,0:T(8,128)S(1)}, f32[6,1024]{1,0:T(8,128)}, u32[]{:S(2)}) copy-start(f32[6,1024]{1,0:T(8,128)} %param.7) | copy-start | bytes 73732
  227.8 3.3 %copy-start.2 = (f32[6,1024]{1,0:T(8,128)S(1)}, f32[6,1024]{1,0:T(8,128)}, u32[]{:S(2)}) copy-start(f32[6,1024]{1,0:T(8,128)} %param.6) | copy-start | bytes 73732
Sparse Core Ops, SparseCore 0:
  11.7 69.0 all-gather.6
  84.5 62.8 all-gather.4
  230.9 31.7 reduce-scatter.3
where the time goes:
time: 275 us
  Pallas kernels  140 us (51%)
  waiting for transfers between devices  79.5 us (29%)
  local copies, waits for them, and re-layouts  24.8 us (9%)
  between operations  14.6 us (5%)
  blocking collectives  11.5 us (4%)
  other arithmetic  5.01 us (2%)
    pallas_call x2, Pallas kernels, add_forces(): pl.pallas_call(forces_kernel, out_shape=jax.ShapeDtypeStruct(acc.shape, j...  140 us
    all_gather x2, waiting for transfers between devices, on_device(): stars = lax.all_gather(piece, ('blk', 'sub'), axis=1, tiled=True)  49.1 us
    unnamed x4, waiting for transfers between devices  30.4 us
    all_gather x2, local copies, waits for them, and re-layouts, on_device(): stars = lax.all_gather(piece, ('blk', 'sub'), axis=1, tiled=True)  6.39 us
    all_gather x1, blocking collectives, on_device(): group_rows = lax.all_gather(targets, 'sub', axis=1, tiled=True)  6.38 us
    unnamed x18, local copies, waits for them, and re-layouts  6.06 us
  transfers between devices with their start and end apart: 3, of which 2 were waited for; matrix products, arithmetic and copies ran while one was open for 5% of the time, Pallas kernels for 25%

commit v1 on v0

--- a/solution.py
+++ b/solution.py
@@ -12,6 +12,8 @@
 
 SOFTEN_SQ = 0.0025
 N_CHUNKS = 2
+ROWS_PER_TRIP = 1
+UNROLL = 8
 
 
 def predict(phase, derivs, elapsed):
@@ -64,41 +66,42 @@
     )
 
 
-def forces_kernel(pairs_ref, rows_ref, stars_ref, acc_ref, out_ref):
+def forces_kernel(trips_ref, rows_ref, stars_ref, acc_ref, out_ref):
     n_rows = out_ref.shape[1]
-    n_blocks = pairs_ref.shape[0]
+    n_blocks = trips_ref.shape[0]
     per_block = n_rows // n_blocks
     n_vregs = stars_ref.shape[1] // SUBLANES
     zero = jnp.zeros((SUBLANES, LANES), jnp.float32)
     out_ref[...] = acc_ref[...]
 
-    def row_scalars(r):
-        return tuple(rows_ref[c * n_rows + r] for c in range(6))
+    def row_vectors(r):
+        return tuple(jnp.full((SUBLANES, LANES), rows_ref[c * n_rows + r], jnp.float32) for c in range(6))
 
     for block in range(n_blocks):
 
-        def pair_body(p, carry, block=block):
-            r0 = block * per_block + 2 * p
-            r1 = r0 + 1
-            row0 = row_scalars(r0)
-            row1 = row_scalars(r1)
+        def trip_body(p, carry, block=block):
+            first = block * per_block + ROWS_PER_TRIP * p
+            rows = [row_vectors(first + k) for k in range(ROWS_PER_TRIP)]
 
             def star_body(j, accs):
                 base = pl.multiple_of(j * SUBLANES, SUBLANES)
                 stars = tuple(stars_ref[c, pl.ds(base, SUBLANES), :] for c in range(7))
-                return pair_sums(row0, stars, accs[:9]) + pair_sums(row1, stars, accs[9:])
+                new = ()
+                for k in range(ROWS_PER_TRIP):
+                    new = new + pair_sums(rows[k], stars, accs[9 * k:9 * k + 9])
+                return new
 
-            accs = lax.fori_loop(0, n_vregs, star_body, (zero,) * 18, unroll=2)
-            for r, part in ((r0, accs[:9]), (r1, accs[9:])):
-                ax, ay, az, jx, jy, jz, qx, qy, qz = part
+            accs = lax.fori_loop(0, n_vregs, star_body, (zero,) * (9 * ROWS_PER_TRIP), unroll=UNROLL)
+            for k in range(ROWS_PER_TRIP):
+                ax, ay, az, jx, jy, jz, qx, qy, qz = accs[9 * k:9 * k + 9]
                 vals = (ax, ay, az, jx - 3.0 * qx, jy - 3.0 * qy, jz - 3.0 * qz)
                 for c in range(6):
-                    out_ref[c, pl.ds(r, 1), :] = out_ref[c, pl.ds(r, 1), :] + jnp.sum(
+                    out_ref[c, pl.ds(first + k, 1), :] = out_ref[c, pl.ds(first + k, 1), :] + jnp.sum(
                         vals[c], axis=0, keepdims=True
                     )
             return carry
 
-        lax.fori_loop(0, pairs_ref[block], pair_body, 0)
+        lax.fori_loop(0, trips_ref[block], trip_body, 0)
 
 
 def add_forces(pairs, rows, stars, acc):
@@ -139,7 +142,7 @@
     dealt = group_rows.reshape(6, n_blocks, per_block, n_sub)
     my_rows = lax.dynamic_slice_in_dim(dealt, me, 1, axis=3).reshape(6, n_blocks * per_block)
     my_counts = jnp.maximum(group_counts - me + n_sub - 1, 0) // n_sub
-    my_pairs = (my_counts + 1) // 2
+    my_trips = (my_counts + ROWS_PER_TRIP - 1) // ROWS_PER_TRIP
 
     n_local = phase.shape[1]
     local_stars = jnp.concatenate([pred_pos, pred_vel, mass[None, :]], axis=0)
@@ -150,7 +153,7 @@
     for chunk in range(n_chunks):
         piece = local_stars[:, chunk * rows_per_chunk:(chunk + 1) * rows_per_chunk, :]
         stars = lax.all_gather(piece, ("blk", "sub"), axis=1, tiled=True)
-        acc = add_forces(my_pairs, my_rows, stars, acc)
+        acc = add_forces(my_trips, my_rows, stars, acc)
     my_forces = jnp.sum(acc, axis=2).reshape(6, n_blocks, per_block, 1)
 
     placed = jnp.where(

time: 275 us -> 243 us (0.88)
  Pallas kernels: 140 us -> 117 us
  waiting for transfers between devices: 79.5 us -> 71.6 us
    pallas_call x2, Pallas kernels: 140 us -> 117 us  [add_forces(): pl.pallas_call(forces_kernel, out_shape=jax.ShapeDtypeStruct(acc.shape, j...]
    unnamed x4, waiting for transfers between devices: 30.4 us -> 18.5 us
    all_gather x2, waiting for transfers between devices: 49.1 us -> 53.1 us  [on_device(): stars = lax.all_gather(piece, ('blk', 'sub'), axis=1, tiled=True)]
  transfers between devices with their start and end apart: 3 -> 3, of which waited for: 2 -> 3; matrix products, arithmetic and copies ran while one was open for 5% -> 6% of each run, Pallas kernels for 25% -> 24%
where the time goes in v1:
time: 243 us; the launch traced here: 245 us
  Pallas kernels  117 us (48%)
  waiting for transfers between devices  71.6 us (29%)
  local copies, waits for them, and re-layouts  24.8 us (10%)
  between operations  14.6 us (6%)
  blocking collectives  11.5 us (5%)
  other arithmetic  5 us (2%)
    pallas_call x2, Pallas kernels, add_forces(): pl.pallas_call(forces_kernel, out_shape=jax.ShapeDtypeStruct(acc.shape, j...  117 us
    all_gather x2, waiting for transfers between devices, on_device(): stars = lax.all_gather(piece, ('blk', 'sub'), axis=1, tiled=True)  53.1 us
    unnamed x4, waiting for transfers between devices  18.5 us
    all_gather x2, local copies, waits for them, and re-layouts, on_device(): stars = lax.all_gather(piece, ('blk', 'sub'), axis=1, tiled=True)  6.39 us
    all_gather x1, blocking collectives, on_device(): group_rows = lax.all_gather(targets, 'sub', axis=1, tiled=True)  6.37 us
    unnamed x18, local copies, waits for them, and re-layouts  6.06 us
    unnamed x1, blocking collectives  5.13 us
  transfers between devices with their start and end apart: 3, of which 3 were waited for; matrix products, arithmetic and copies ran while one was open for 6% of the time, Pallas kernels for 24%

profile of v1, /device:TPU:1, one launch (start us, length us, event | category | flops | bytes accessed | tf_op | source)
XLA Modules:
  0.0 244.6 jit_solution(8091755118588295500)
XLA Ops:
  7.2 0.7 multiply_multiply_fusion.1
  7.9 0.9 multiply_add_fusion
  8.8 0.7 pad_maximum_fusion
  9.5 0.6 fusion.2
  10.2 0.7 all-gather.5.cloned.1.call-update
  11.0 1.2 dynamic-slice
  12.9 0.8 bitcast_dynamic-update-slice_fusion
  13.6 5.1 %all-reduce = s32[12]{0:T(128)S(1)} all-reduce(s32[12]{0:T(128)S(1)} %bitcast_dynamic-update-slice_fusion), channel_id=2, replica_groups=mesh['blk'=32,'sub'=4] {'sub'}, use_global_device_ids=true, to_apply=%add | all-reduce | flops 12 | bytes 96
  19.2 0.8 reshape.106
  20.0 1.2 gather_fusion.1
  21.2 0.7 gather_fusion.3
  21.9 0.7 gather_fusion
  22.7 6.4 %all-gather.1 = f32[4,192,6]{1,2,0:T(8,128)S(1)} all-gather(f32[1,192,6]{1,2,0:T(8,128)S(1)} %maximum_bitcast_fusion), channel_id=1, replica_groups=mesh['blk'=32,'sub'=4] {'sub'}, dimensions={0}, use_global_device_ids=true | all-gather | bytes 23040 | tf_op jit(solution)/shard_map/all_gather | solution.py:138
  30.3 0.7 reshape_reshape.4.rows_ref
  31.7 49.1 %all-gather.7.cloned.1.call-done = f32[7,512,128]{2,0,1:T(8,128)} async-done(((f32[7,4,128]{2,0,1:T(8,128)}), f32[7,512,128]{2,0,1:T(8,128)}) %all-gather.7.cloned.1.call-update) | async-done | bytes 1835024 | tf_op jit(solution)/shard_map/all_gather | solution.py:155
  80.8 3.2 %copy.190.stars_ref = f32[7,512,128]{2,1,0:T(8,128)} copy(f32[7,512,128]{2,0,1:T(8,128)} %all-gather.7.cloned.1.call-done) | data formatting | bytes 3670016 | tf_op jit(solution)/shard_map/all_gather | solution.py:155
  84.0 0.9 broadcast_in_dim.69.acc_ref
  84.9 58.5 %shard_map.85.acc_ref = f32[6,192,128]{2,1,0:T(8,128)} custom-call(s32[12]{0:T(128)} %bitcast_select_fusion.trips_ref, f32[1152]{0:T(1024)} %reshape_reshape.4.rows_ref, f32[7,512,128]{2,1,0:T(8,128)} %copy.190.stars_ref, f32[6,192,128]{2,1,0:T(8,128)} %broadcast_in_dim.69.acc_ref), custom_call_target="tpu_custom_call", output_to_operand_aliasing={{}: (3, {})} | custom-call | flops 503316480 | bytes 3014656 | tf_op jit(solution)/shard_map/pallas_call | solution.py:110
  143.4 4.0 %all-gather.5.cloned.1.call-done = f32[7,512,128]{2,0,1:T(8,128)} async-done(((f32[7,4,128]{2,0,1:T(8,128)}), f32[7,512,128]{2,0,1:T(8,128)}) %all-gather.5.cloned.1.call-update) | async-done | bytes 1835024 | tf_op jit(solution)/shard_map/all_gather | solution.py:155
  147.4 3.2 %copy.191.stars_ref = f32[7,512,128]{2,1,0:T(8,128)} copy(f32[7,512,128]{2,0,1:T(8,128)} %all-gather.5.cloned.1.call-done) | data formatting | bytes 3670016 | tf_op jit(solution)/shard_map/all_gather | solution.py:155
  150.6 58.5 %shard_map.86 = f32[6,192,128]{2,1,0:T(8,128)} custom-call(s32[12]{0:T(128)} %bitcast_select_fusion.trips_ref, f32[1152]{0:T(1024)} %reshape_reshape.4.rows_ref, f32[7,512,128]{2,1,0:T(8,128)} %copy.191.stars_ref, f32[6,192,128]{2,1,0:T(8,128)} %shard_map.85.acc_ref), custom_call_target="tpu_custom_call", output_to_operand_aliasing={{}: (3, {})} | custom-call | flops 503316480 | bytes 3014656 | tf_op jit(solution)/shard_map/pallas_call | solution.py:110
  209.1 1.4 reduce_sum.9
  211.1 0.9 copy.200
  212.6 0.7 gather_fusion.2
  213.4 0.7 gather_fusion.4
  214.3 17.8 %reduce-scatter.4.cloned.1.call-done = f32[192,6]{1,0:T(8,128)} async-done(((f32[768,6]{1,0:T(8,128)}), f32[192,6]{1,0:T(8,128)}) %reduce-scatter.4.cloned.1.call-update) | async-done | bytes 4624
  232.0 1.0 copy.201
  233.3 1.2 scatter_fusion.1
  234.5 0.8 copy.199
  235.4 1.2 scatter_fusion
  236.7 0.8 copy.198
  237.5 0.6 broadcast_select_fusion.1
  (46 shorter events, 4.4 us)
Async XLA Ops:
  7.2 12.8 %copy-start = (f32[1024]{0:T(1024)S(1)}, f32[1024]{0:T(1024)}, u32[]{:S(2)}) copy-start(f32[1024]{0:T(1024)} %param.9) | copy-start | bytes 12292
  7.2 73.6 %all-gather.7.cloned.1.call-start = ((), (), s32[]{:S(2)}) async-start(), calls=%async_computation.2 | async-start | bytes 2113536 | tf_op jit(solution)/shard_map/all_gather | solution.py:155
  10.1 137.3 %all-gather.5.cloned.1.call-start = ((), (), s32[]{:S(2)}) async-start(), calls=%async_computation.1 | async-start | bytes 2113536 | tf_op jit(solution)/shard_map/all_gather | solution.py:155
  10.9 221.1 %reduce-scatter.4.cloned.1.call-start = ((), (), s32[]{:S(2)}) async-start(), calls=%async_computation.3 | async-start | bytes 491520
  209.1 3.0 %copy-start.3 = (s32[3,1]{0,1:T(1,128)S(1)}, s32[3,1]{0,1:T(1,128)}, u32[]{:S(2)}) copy-start(s32[3,1]{0,1:T(1,128)} %param.11) | copy-start | bytes 40
  209.1 3.1 %copy-start.1 = (f32[6,1024]{1,0:T(8,128)S(1)}, f32[6,1024]{1,0:T(8,128)}, u32[]{:S(2)}) copy-start(f32[6,1024]{1,0:T(8,128)} %param.7) | copy-start | bytes 73732
  209.1 3.3 %copy-start.2 = (f32[6,1024]{1,0:T(8,128)S(1)}, f32[6,1024]{1,0:T(8,128)}, u32[]{:S(2)}) copy-start(f32[6,1024]{1,0:T(8,128)} %param.6) | copy-start | bytes 73732
Sparse Core Ops, SparseCore 0:
  11.7 69.0 all-gather.6
  84.5 62.8 all-gather.4
  212.2 19.7 reduce-scatter.3

commit v2 on v1

--- a/solution.py
+++ b/solution.py
@@ -11,7 +11,8 @@
 LANES = 128
 
 SOFTEN_SQ = 0.0025
-N_CHUNKS = 2
+MIN_ROWS = 64
+VPU_COST = 5000
 ROWS_PER_TRIP = 1
 UNROLL = 8
 
@@ -119,11 +120,20 @@
         out_specs=pl.BlockSpec(memory_space=pltpu.VMEM),
         input_output_aliases={3: 0},
         cost_estimate=pl.CostEstimate(
-            flops=40 * n_rows * n_stars,
+            flops=VPU_COST * n_rows * n_stars,
             transcendentals=n_rows * n_stars,
             bytes_accessed=4 * (stars.size + 2 * acc.size),
         ),
     )(pairs, rows.reshape(-1), stars, acc)
+
+
+def xor_swap(x, axis, bit):
+    n = lax.axis_size(axis)
+    return lax.ppermute(x, axis, [(i, i ^ bit) for i in range(n)])
+
+
+def in_order(mine, theirs, upper):
+    return jnp.where(upper, jnp.concatenate([theirs, mine], axis=1), jnp.concatenate([mine, theirs], axis=1))
 
 
 def on_device(phase, derivs, mass, elapsed, active_slots, active_counts):
@@ -132,34 +142,63 @@
     live_grid = lax.broadcasted_iota(jnp.int32, (LEVELS, LCAP), 1) < active_counts
     is_live = live_grid.reshape(-1)
     targets = jnp.concatenate([pred_pos[:, slot_rows], pred_vel[:, slot_rows]], axis=0)
+    n_slots = targets.shape[1]
 
     n_sub = lax.axis_size("sub")
     me = lax.axis_index("sub")
-    group_rows = lax.all_gather(targets, "sub", axis=1, tiled=True)
-    group_counts = lax.all_gather(active_counts.reshape(-1), "sub", axis=0, tiled=True)
+    count_row = jnp.zeros((1, n_slots), jnp.float32).at[0, :LEVELS].set(
+        active_counts.reshape(-1).astype(jnp.float32)
+    )
+    group = jnp.concatenate([targets, count_row], axis=0)
+    bit = 1
+    while bit < n_sub:
+        group = in_order(group, xor_swap(group, "sub", bit), (me & bit) != 0)
+        bit *= 2
+    group_rows = group[:6]
+    group_counts = group[6].reshape(n_sub, n_slots)[:, :LEVELS].reshape(-1).astype(jnp.int32)
+
     n_blocks = group_counts.shape[0]
     per_block = LCAP // n_sub
+    offsets = (me - jnp.arange(n_blocks, dtype=jnp.int32)) % n_sub
     dealt = group_rows.reshape(6, n_blocks, per_block, n_sub)
-    my_rows = lax.dynamic_slice_in_dim(dealt, me, 1, axis=3).reshape(6, n_blocks * per_block)
-    my_counts = jnp.maximum(group_counts - me + n_sub - 1, 0) // n_sub
+    my_rows = jnp.take_along_axis(dealt, offsets.reshape(1, n_blocks, 1, 1), axis=3)
+    my_rows = my_rows.reshape(6, n_blocks * per_block)
+    my_counts = jnp.maximum(group_counts - offsets + n_sub - 1, 0) // n_sub
     my_trips = (my_counts + ROWS_PER_TRIP - 1) // ROWS_PER_TRIP
 
     n_local = phase.shape[1]
-    local_stars = jnp.concatenate([pred_pos, pred_vel, mass[None, :]], axis=0)
-    local_stars = local_stars.reshape(7, n_local // LANES, LANES)
-    n_chunks = N_CHUNKS
-    rows_per_chunk = local_stars.shape[1] // n_chunks
+    have = jnp.concatenate([pred_pos, pred_vel, mass[None, :]], axis=0)
+    have = have.reshape(7, n_local // LANES, LANES)
+    my_rows, my_trips, have = lax.optimization_barrier((my_rows, my_trips, have))
     acc = jnp.zeros((6, n_blocks * per_block, LANES), jnp.float32)
-    for chunk in range(n_chunks):
-        piece = local_stars[:, chunk * rows_per_chunk:(chunk + 1) * rows_per_chunk, :]
-        stars = lax.all_gather(piece, ("blk", "sub"), axis=1, tiled=True)
-        acc = add_forces(my_trips, my_rows, stars, acc)
+    stages = []
+    bit = 1
+    while bit < lax.axis_size("blk"):
+        stages.append(("blk", bit))
+        bit *= 2
+    bit = n_sub // 2
+    while bit >= 1:
+        stages.append(("sub", bit))
+        bit //= 2
+    pending = None
+    for axis, bit in stages:
+        theirs = xor_swap(have, axis, bit)
+        if pending is None and have.shape[1] + theirs.shape[1] >= MIN_ROWS:
+            pending = jnp.concatenate([have, theirs], axis=1)
+        elif pending is not None:
+            pending = theirs
+        if pending is not None:
+            acc = add_forces(my_trips, my_rows, pending, acc)
+        have = jnp.concatenate([have, theirs], axis=1)
     my_forces = jnp.sum(acc, axis=2).reshape(6, n_blocks, per_block, 1)
 
-    placed = jnp.where(
-        lax.broadcasted_iota(jnp.int32, (1, 1, 1, n_sub), 3) == me, my_forces, 0.0
-    ).reshape(6, n_blocks * LCAP)
-    new_forces = lax.psum_scatter(placed, "sub", scatter_dimension=1, tiled=True)
+    lane = lax.broadcasted_iota(jnp.int32, (1, n_blocks, 1, n_sub), 3)
+    placed = jnp.where(lane == offsets.reshape(1, n_blocks, 1, 1), my_forces, 0.0)
+    placed = placed.reshape(6, n_sub, n_slots)
+    new_forces = lax.dynamic_index_in_dim(placed, me, axis=1, keepdims=False)
+    for step in range(1, n_sub):
+        outgoing = lax.dynamic_index_in_dim(placed, me ^ step, axis=1, keepdims=False)
+        new_forces = new_forces + xor_swap(outgoing, "sub", step)
 
     shaped_forces = new_forces.reshape(6, LEVELS, LCAP)
     active_forces = jnp.where(live_grid[None, :, :], shaped_forces, jnp.zeros_like(shaped_forces))

time: 243 us -> 181 us (0.74)
  the two profiles are of different devices: /device:TPU:1 before, /device:TPU:39 now
where the time goes in v2:
time: 181 us; the launch traced here: 178 us
  Pallas kernels  127 us (70%)
  local copies, waits for them, and re-layouts  20.4 us (11%)
  starting transfers between devices  18 us (10%)
  other arithmetic  6.41 us (4%)
  waiting for transfers between devices  5.29 us (3%)
    pallas_call x5, Pallas kernels, add_forces(): pl.pallas_call(forces_kernel, out_shape=jax.ShapeDtypeStruct(acc.shape, j...  127 us
    ppermute x12, starting transfers between devices, xor_swap(): return lax.ppermute(x, axis, [(i, i ^ bit) for i in range(n)])  18 us
    unnamed x31, local copies, waits for them, and re-layouts  5.43 us
    ppermute x12, waiting for transfers between devices, xor_swap(): return lax.ppermute(x, axis, [(i, i ^ bit) for i in range(n)])  5.29 us
  transfers between devices with their start and end apart: 12, of which 3 were waited for; matrix products, arithmetic and copies ran while one was open for 4% of the time, Pallas kernels for 39%

profile of v2, /device:TPU:39, one launch (start us, length us, event | category | flops | bytes accessed | tf_op | source)
XLA Modules:
  0.0 177.7 jit_solution(8504933270570815334)
XLA Ops:
  1.3 0.8 reshape.258
  2.8 0.9 multiply_add_fusion
  3.8 0.7 gather_fusion
  5.6 1.3 fusion.4
  7.0 0.8 collective-permute-start
  7.7 1.2 gather_fusion.1
  9.1 1.3 collective-permute-start.1
  10.6 1.1 collective-permute-done.1
  14.4 2.9 %collective-permute-start.2 = (f32[7,8,128]{2,1,0:T(8,128)S(1)}, f32[7,8,128]{2,1,0:T(8,128)S(1)}, u32[]{:S(2)}, u32[]{:S(2)}) collective-permute-start(f32[7,8,128]{2,1,0:T(8,128)S(1)} %pad_maximum_fusion.2), channel_id=1, source_target_pairs={{0,4},{4,0},{8,12},{12,8},{16,20},{20,16},{24,28},{28,24},{32,36},... | collective-permute-start | bytes 86024 | tf_op jit(solution)/shard_map/ppermute | solution.py:132
  19.6 2.4 %collective-permute-done.3 = f32[7,16,128]{2,1,0:T(8,128)S(1)} collective-permute-done((f32[7,16,128]{2,1,0:T(8,128)S(1)}, f32[7,16,128]{2,1,0:T(8,128)S(1)}, u32[]{:S(2)}, u32[]{:S(2)}) %collective-permute-start.3) | collective-permute-done | bytes 57376 | tf_op jit(solution)/shard_map/ppermute | solution.py:132
  22.0 2.8 %collective-permute-start.4 = (f32[7,32,128]{2,1,0:T(8,128)S(1)}, f32[7,32,128]{2,1,0:T(8,128)S(1)}, u32[]{:S(2)}, u32[]{:S(2)}) collective-permute-start(f32[7,32,128]{2,1,0:T(8,128)S(1)} %pad_maximum_fusion), channel_id=1, source_target_pairs={{0,16},{4,20},{8,24},{12,28},{16,0},{20,4},{24,8},{28,12},{32,48},... | collective-permute-start | bytes 344072 | tf_op jit(solution)/shard_map/ppermute | solution.py:132
  25.4 1.8 %collective-permute-done.4 = f32[7,32,128]{2,1,0:T(8,128)S(1)} collective-permute-done((f32[7,32,128]{2,1,0:T(8,128)S(1)}, f32[7,32,128]{2,1,0:T(8,128)S(1)}, u32[]{:S(2)}, u32[]{:S(2)}) %collective-permute-start.4) | collective-permute-done | bytes 114720 | tf_op jit(solution)/shard_map/ppermute | solution.py:132
  28.4 0.9 broadcast_in_dim.86.acc_ref
  29.3 10.5 %shard_map.85.acc_ref = f32[6,192,128]{2,1,0:T(8,128)} custom-call(s32[12]{0:T(128)} %get-tuple-element.18.trips_ref, f32[1152]{0:T(1024)} %reshape.261.rows_ref, f32[7,64,128]{2,1,0:T(8,128)} %copy-done.7, f32[6,192,128]{2,1,0:T(8,128)} %broadcast_in_dim.86.acc_ref), custom_call_target="tpu_custom_call", output_to_operand_aliasing={{}: (3, {})} | custom-call | flops 7864320000 | bytes 1409024 | tf_op jit(solution)/shard_map/pallas_call | solution.py:111
  39.7 0.8 constant_dynamic-update-slice_fusion.10
  41.1 10.5 %shard_map.86.acc_ref = f32[6,192,128]{2,1,0:T(8,128)} custom-call(s32[12]{0:T(128)} %get-tuple-element.18.trips_ref, f32[1152]{0:T(1024)} %reshape.261.rows_ref, f32[7,64,128]{2,1,0:T(8,128)} %copy-done.3, f32[6,192,128]{2,1,0:T(8,128)} %shard_map.85.acc_ref), custom_call_target="tpu_custom_call", output_to_operand_aliasing={{}: (3, {})} | custom-call | flops 7864320000 | bytes 1409024 | tf_op jit(solution)/shard_map/pallas_call | solution.py:111
  51.6 1.0 constant_dynamic-update-slice_fusion.9
  52.6 1.3 collective-permute-start.7
  53.8 17.5 %shard_map.87.acc_ref = f32[6,192,128]{2,1,0:T(8,128)} custom-call(s32[12]{0:T(128)} %get-tuple-element.18.trips_ref, f32[1152]{0:T(1024)} %reshape.261.rows_ref, f32[7,128,128]{2,1,0:T(8,128)} %copy-done.2, f32[6,192,128]{2,1,0:T(8,128)} %shard_map.86.acc_ref), custom_call_target="tpu_custom_call", output_to_operand_aliasing={{}: (3, {})} | custom-call | flops 15728640000 | bytes 1638400 | tf_op jit(solution)/shard_map/pallas_call | solution.py:111
  71.4 1.1 constant_dynamic-update-slice_fusion.15
  72.4 5.3 %collective-permute-start.8 = (f32[7,512,128]{2,1,0:T(8,128)}, f32[7,512,128]{2,1,0:T(8,128)}, u32[]{:S(2)}, u32[]{:S(2)}) collective-permute-start(f32[7,512,128]{2,1,0:T(8,128)} %constant_dynamic-update-slice_fusion.15), channel_id=1, source_target_pairs={{0,1},{1,0},{2,3},{3,2},{4,5},{5,4},{6,7},{7,6},{8,9},{9,8},{10,11... | collective-permute-start | bytes 5505032 | tf_op jit(solution)/shard_map/ppermute | solution.py:132
  77.7 30.8 %shard_map.88.acc_ref = f32[6,192,128]{2,1,0:T(8,128)} custom-call(s32[12]{0:T(128)} %get-tuple-element.18.trips_ref, f32[1152]{0:T(1024)} %reshape.261.rows_ref, f32[7,256,128]{2,1,0:T(8,128)} %copy-done.1, f32[6,192,128]{2,1,0:T(8,128)} %shard_map.87.acc_ref), custom_call_target="tpu_custom_call", output_to_operand_aliasing={{}: (3, {})} | custom-call | flops 31457280000 | bytes 2097152 | tf_op jit(solution)/shard_map/pallas_call | solution.py:111
  108.5 57.4 %shard_map.89 = f32[6,192,128]{2,1,0:T(8,128)} custom-call(s32[12]{0:T(128)} %get-tuple-element.18.trips_ref, f32[1152]{0:T(1024)} %reshape.261.rows_ref, f32[7,512,128]{2,1,0:T(8,128)} %collective-permute-done.8.stars_ref, f32[6,192,128]{2,1,0:T(8,128)} %shard_map.88.acc_ref), custom_call_target="tpu_custom_call", output_to_operand_aliasing={{}: (3, {})} | custom-call | flops 62914560000 | bytes 3014656 | tf_op jit(solution)/shard_map/pallas_call | solution.py:111
  165.9 1.4 reduce_sum.9
  167.9 1.0 collective-permute-start.10
  168.9 1.5 collective-permute-start.11
  171.0 0.7 gather_fusion.2
  171.8 0.7 gather_fusion.4
  172.8 1.2 scatter_fusion.1
  174.0 0.8 copy.159
  175.1 1.2 scatter_fusion
  176.3 0.8 copy.158
  (97 shorter events, 12.7 us)
Async XLA Ops:
  0.6 7.1 %copy-start = (f32[1024]{0:T(1024)S(1)}, f32[1024]{0:T(1024)}, u32[]{:S(2)}) copy-start(f32[1024]{0:T(1024)} %param.11) | copy-start | bytes 12292
  0.6 8.4 %copy-start.6 = (f32[1024]{0:T(1024)S(1)}, f32[1024]{0:T(1024)}, u32[]{:S(2)}) copy-start(f32[1024]{0:T(1024)} %param.10) | copy-start | bytes 12292
  7.0 2.1 %collective-permute-start = (f32[7,192]{1,0:T(8,128)S(1)}, f32[7,192]{1,0:T(8,128)S(1)}, u32[]{:S(2)}, u32[]{:S(2)}) collective-permute-start(f32[7,192]{1,0:T(8,128)S(1)} %pad_maximum_fusion.3), channel_id=1, source_target_pairs={{0,1},{1,0},{2,3},{3,2},{4,5},{5,4},{6,7},{7,6},{8,9},{9,8},{10,11... | collective-permute-start | bytes 16136 | tf_op jit(solution)/shard_map/ppermute | solution.py:132
  9.1 2.6 %collective-permute-start.1 = (f32[7,384]{1,0:T(8,128)S(1)}, f32[7,384]{1,0:T(8,128)S(1)}, u32[]{:S(2)}, u32[]{:S(2)}) collective-permute-start(f32[7,384]{1,0:T(8,128)S(1)} %maximum_select_fusion.1), channel_id=1, source_target_pairs={{0,2},{1,3},{2,0},{3,1},{4,6},{5,7},{6,4},{7,5},{8,10},{9,11},{10,... | collective-permute-start | bytes 32264 | tf_op jit(solution)/shard_map/ppermute | solution.py:132
  14.4 4.4 %collective-permute-start.2 = (f32[7,8,128]{2,1,0:T(8,128)S(1)}, f32[7,8,128]{2,1,0:T(8,128)S(1)}, u32[]{:S(2)}, u32[]{:S(2)}) collective-permute-start(f32[7,8,128]{2,1,0:T(8,128)S(1)} %pad_maximum_fusion.2), channel_id=1, source_target_pairs={{0,4},{4,0},{8,12},{12,8},{16,20},{20,16},{24,28},{28,24},{32,36},... | collective-permute-start | bytes 86024 | tf_op jit(solution)/shard_map/ppermute | solution.py:132
  18.9 3.1 %collective-permute-start.3 = (f32[7,16,128]{2,1,0:T(8,128)S(1)}, f32[7,16,128]{2,1,0:T(8,128)S(1)}, u32[]{:S(2)}, u32[]{:S(2)}) collective-permute-start(f32[7,16,128]{2,1,0:T(8,128)S(1)} %pad_maximum_fusion.1), channel_id=1, source_target_pairs={{0,8},{4,12},{8,0},{12,4},{16,24},{20,28},{24,16},{28,20},{32,40},... | collective-permute-start | bytes 172040 | tf_op jit(solution)/shard_map/ppermute | solution.py:132
  22.0 5.2 %collective-permute-start.4 = (f32[7,32,128]{2,1,0:T(8,128)S(1)}, f32[7,32,128]{2,1,0:T(8,128)S(1)}, u32[]{:S(2)}, u32[]{:S(2)}) collective-permute-start(f32[7,32,128]{2,1,0:T(8,128)S(1)} %pad_maximum_fusion), channel_id=1, source_target_pairs={{0,16},{4,20},{8,24},{12,28},{16,0},{20,4},{24,8},{28,12},{32,48},... | collective-permute-start | bytes 344072 | tf_op jit(solution)/shard_map/ppermute | solution.py:132
  27.9 1.4 copy-start.7
  27.9 11.9 %collective-permute-start.5 = (f32[7,64,128]{2,1,0:T(8,128)S(1)}, f32[7,64,128]{2,1,0:T(8,128)S(1)}, u32[]{:S(2)}, u32[]{:S(2)}) collective-permute-start(f32[7,64,128]{2,1,0:T(8,128)S(1)} %get-tuple-element.55.stars_ref), channel_id=1, source_target_pairs={{0,32},{4,36},{8,40},{12,44},{16,48},{20,52},{24,56},{28,60},{32,0... | collective-permute-start | bytes 688136 | tf_op jit(solution)/shard_map/ppermute | solution.py:132
  39.7 1.4 copy-start.3
  40.6 11.1 %collective-permute-start.6 = (f32[7,128,128]{2,1,0:T(8,128)S(1)}, f32[7,128,128]{2,1,0:T(8,128)S(1)}, u32[]{:S(2)}, u32[]{:S(2)}) collective-permute-start(f32[7,128,128]{2,1,0:T(8,128)S(1)} %get-tuple-element.51), channel_id=1, source_target_pairs={{0,64},{4,68},{8,72},{12,76},{16,80},{20,84},{24,88},{28,92},{32,9... | collective-permute-start | bytes 1376264 | tf_op jit(solution)/shard_map/ppermute | solution.py:132
  51.6 2.2 %copy-start.2 = (f32[7,128,128]{2,1,0:T(8,128)}, f32[7,128,128]{2,1,0:T(8,128)S(1)}, u32[]{:S(2)}) copy-start(f32[7,128,128]{2,1,0:T(8,128)S(1)} %collective-permute-done.6.stars_ref) | copy-start | bytes 1376260
  52.6 18.8 %collective-permute-start.7 = (f32[7,256,128]{2,1,0:T(8,128)S(1)}, f32[7,256,128]{2,1,0:T(8,128)S(1)}, u32[]{:S(2)}, u32[]{:S(2)}) collective-permute-start(f32[7,256,128]{2,1,0:T(8,128)S(1)} %get-tuple-element.47), channel_id=1, source_target_pairs={{0,2},{1,3},{2,0},{3,1},{4,6},{5,7},{6,4},{7,5},{8,10},{9,11},{10,... | collective-permute-start | bytes 2752520 | tf_op jit(solution)/shard_map/ppermute | solution.py:132
  71.4 6.3 %copy-start.1 = (f32[7,256,128]{2,1,0:T(8,128)}, f32[7,256,128]{2,1,0:T(8,128)S(1)}, u32[]{:S(2)}) copy-start(f32[7,256,128]{2,1,0:T(8,128)S(1)} %collective-permute-done.7.stars_ref) | copy-start | bytes 2752516
  72.4 36.0 %collective-permute-start.8 = (f32[7,512,128]{2,1,0:T(8,128)}, f32[7,512,128]{2,1,0:T(8,128)}, u32[]{:S(2)}, u32[]{:S(2)}) collective-permute-start(f32[7,512,128]{2,1,0:T(8,128)} %constant_dynamic-update-slice_fusion.15), channel_id=1, source_target_pairs={{0,1},{1,0},{2,3},{3,2},{4,5},{5,4},{6,7},{7,6},{8,9},{9,8},{10,11... | collective-permute-start | bytes 5505032 | tf_op jit(solution)/shard_map/ppermute | solution.py:132
  165.9 4.5 %copy-start.8 = (s32[3,1]{0,1:T(1,128)S(1)}, s32[3,1]{0,1:T(1,128)}, u32[]{:S(2)}) copy-start(s32[3,1]{0,1:T(1,128)} %param.13) | copy-start | bytes 40
  165.9 4.6 %copy-start.4 = (f32[6,1024]{1,0:T(8,128)S(1)}, f32[6,1024]{1,0:T(8,128)}, u32[]{:S(2)}) copy-start(f32[6,1024]{1,0:T(8,128)} %param.9) | copy-start | bytes 73732
  165.9 4.8 %copy-start.5 = (f32[6,1024]{1,0:T(8,128)S(1)}, f32[6,1024]{1,0:T(8,128)}, u32[]{:S(2)}) copy-start(f32[6,1024]{1,0:T(8,128)} %param.8) | copy-start | bytes 73732
  167.9 4.7 %collective-permute-start.10 = (f32[6,192]{1,0:T(8,128)S(1)}, f32[6,192]{1,0:T(8,128)S(1)}, u32[]{:S(2)}, u32[]{:S(2)}) collective-permute-start(f32[6,192]{1,0:T(8,128)S(1)} %bitcast.59), channel_id=1, source_target_pairs={{0,2},{1,3},{2,0},{3,1},{4,6},{5,7},{6,4},{7,5},{8,10},{9,11},{10,... | collective-permute-start | bytes 13832 | tf_op jit(solution)/shard_map/ppermute | solution.py:132
  168.9 3.7 %collective-permute-start.11 = (f32[6,192]{1,0:T(8,128)S(1)}, f32[6,192]{1,0:T(8,128)S(1)}, u32[]{:S(2)}, u32[]{:S(2)}) collective-permute-start(f32[6,192]{1,0:T(8,128)S(1)} %bitcast.60), channel_id=1, source_target_pairs={{0,3},{1,2},{2,1},{3,0},{4,7},{5,6},{6,5},{7,4},{8,11},{9,10},{10,... | collective-permute-start | bytes 13832 | tf_op jit(solution)/shard_map/ppermute | solution.py:132
  170.4 2.2 %collective-permute-start.9 = (f32[6,192]{1,0:T(8,128)S(1)}, f32[6,192]{1,0:T(8,128)S(1)}, u32[]{:S(2)}, u32[]{:S(2)}) collective-permute-start(f32[6,192]{1,0:T(8,128)S(1)} %bitcast.61), channel_id=1, source_target_pairs={{0,1},{1,0},{2,3},{3,2},{4,5},{5,4},{6,7},{7,6},{8,9},{9,8},{10,11... | collective-permute-start | bytes 13832 | tf_op jit(solution)/shard_map/ppermute | solution.py:132

commit v3 on v2

--- a/solution.py
+++ b/solution.py
@@ -76,7 +76,7 @@
     out_ref[...] = acc_ref[...]
 
     def row_vectors(r):
-        return tuple(jnp.full((SUBLANES, LANES), rows_ref[c * n_rows + r], jnp.float32) for c in range(6))
+        return tuple(rows_ref[c * n_rows + r] for c in range(6))
 
     for block in range(n_blocks):
 
@@ -169,7 +169,6 @@
     n_local = phase.shape[1]
     have = jnp.concatenate([pred_pos, pred_vel, mass[None, :]], axis=0)
     have = have.reshape(7, n_local // LANES, LANES)
-    my_rows, my_trips, have = lax.optimization_barrier((my_rows, my_trips, have))
     acc = jnp.zeros((6, n_blocks * per_block, LANES), jnp.float32)
     stages = []
     bit = 1

time: 181 us -> 184 us (1.017)
  the two profiles are of different devices: /device:TPU:39 before, /device:TPU:17 now
where the time goes in v3:
time: 184 us; the launch traced here: 182 us
  Pallas kernels  132 us (72%)
  local copies, waits for them, and re-layouts  19.5 us (11%)
  starting transfers between devices  18.8 us (10%)
  other arithmetic  7.88 us (4%)
  waiting for transfers between devices  3.62 us (2%)
    pallas_call x5, Pallas kernels, add_forces(): pl.pallas_call(forces_kernel, out_shape=jax.ShapeDtypeStruct(acc.shape, j...  132 us
    ppermute x12, starting transfers between devices, xor_swap(): return lax.ppermute(x, axis, [(i, i ^ bit) for i in range(n)])  18.8 us
    unnamed x30, local copies, waits for them, and re-layouts  4.81 us
  transfers between devices with their start and end apart: 12, of which 3 were waited for; matrix products, arithmetic and copies ran while one was open for 8% of the time, Pallas kernels for 39%

profile of v3, /device:TPU:17, one launch (start us, length us, event | category | flops | bytes accessed | tf_op | source)
XLA Modules:
  0.0 182.3 jit_solution(803184772482939379)
XLA Ops:
  1.4 0.9 multiply_add_fusion
  2.3 1.3 constant_dynamic-update-slice_fusion.10
  4.7 0.8 reshape.250
  7.0 1.3 fusion.4
  8.4 1.0 collective-permute-start
  9.4 1.2 gather_fusion.1
  10.8 2.0 %collective-permute-start.1 = (f32[7,384]{1,0:T(8,128)S(1)}, f32[7,384]{1,0:T(8,128)S(1)}, u32[]{:S(2)}, u32[]{:S(2)}) collective-permute-start(f32[7,384]{1,0:T(8,128)S(1)} %maximum_select_fusion.1), channel_id=1, source_target_pairs={{0,2},{1,3},{2,0},{3,1},{4,6},{5,7},{6,4},{7,5},{8,10},{9,11},{10,... | collective-permute-start | bytes 32264 | tf_op jit(solution)/shard_map/ppermute | solution.py:132
  13.0 0.9 collective-permute-done.1
  17.3 1.7 collective-permute-start.3
  19.6 1.0 collective-permute-done.3
  20.6 3.5 %collective-permute-start.4 = (f32[7,32,128]{2,1,0:T(8,128)S(1)}, f32[7,32,128]{2,1,0:T(8,128)S(1)}, u32[]{:S(2)}, u32[]{:S(2)}) collective-permute-start(f32[7,32,128]{2,1,0:T(8,128)S(1)} %pad_maximum_fusion.1), channel_id=1, source_target_pairs={{0,16},{4,20},{8,24},{12,28},{16,0},{20,4},{24,8},{28,12},{32,48},... | collective-permute-start | bytes 344072 | tf_op jit(solution)/shard_map/ppermute | solution.py:132
  24.7 1.7 collective-permute-done.4
  26.5 1.3 collective-permute-start.5
  27.8 0.9 broadcast_in_dim.83.acc_ref
  28.7 10.9 %shard_map.85.acc_ref = f32[6,192,128]{2,1,0:T(8,128)} custom-call(s32[12]{0:T(128)} %and_select_fusion.1.trips_ref, f32[1152]{0:T(1024)} %reshape.320.rows_ref, f32[7,64,128]{2,1,0:T(8,128)} %copy-done.4, f32[6,192,128]{2,1,0:T(8,128)} %broadcast_in_dim.83.acc_ref), custom_call_target="tpu_custom_call", output_to_operand_aliasing={{}: (3, {})} | custom-call | flops 7864320000 | bytes 1409024 | tf_op jit(solution)/shard_map/pallas_call | solution.py:111
  40.2 0.8 constant_dynamic-update-slice_fusion.6
  41.0 2.2 %collective-permute-start.6 = (f32[7,128,128]{2,1,0:T(8,128)S(1)}, f32[7,128,128]{2,1,0:T(8,128)S(1)}, u32[]{:S(2)}, u32[]{:S(2)}) collective-permute-start(f32[7,128,128]{2,1,0:T(8,128)S(1)} %get-tuple-element.45), channel_id=1, source_target_pairs={{0,64},{4,68},{8,72},{12,76},{16,80},{20,84},{24,88},{28,92},{32,9... | collective-permute-start | bytes 1376264 | tf_op jit(solution)/shard_map/ppermute | solution.py:132
  43.2 10.9 %shard_map.86.acc_ref = f32[6,192,128]{2,1,0:T(8,128)} custom-call(s32[12]{0:T(128)} %and_select_fusion.1.trips_ref, f32[1152]{0:T(1024)} %reshape.320.rows_ref, f32[7,64,128]{2,1,0:T(8,128)} %copy-done.3, f32[6,192,128]{2,1,0:T(8,128)} %shard_map.85.acc_ref), custom_call_target="tpu_custom_call", output_to_operand_aliasing={{}: (3, {})} | custom-call | flops 7864320000 | bytes 1409024 | tf_op jit(solution)/shard_map/pallas_call | solution.py:111
  54.1 0.9 constant_dynamic-update-slice_fusion.5
  55.0 1.5 collective-permute-start.7
  56.5 17.8 %shard_map.87.acc_ref = f32[6,192,128]{2,1,0:T(8,128)} custom-call(s32[12]{0:T(128)} %and_select_fusion.1.trips_ref, f32[1152]{0:T(1024)} %reshape.320.rows_ref, f32[7,128,128]{2,1,0:T(8,128)} %copy-done.2, f32[6,192,128]{2,1,0:T(8,128)} %shard_map.86.acc_ref), custom_call_target="tpu_custom_call", output_to_operand_aliasing={{}: (3, {})} | custom-call | flops 15728640000 | bytes 1638400 | tf_op jit(solution)/shard_map/pallas_call | solution.py:111
  74.3 1.0 constant_dynamic-update-slice_fusion.11
  75.3 3.6 %collective-permute-start.8 = (f32[7,512,128]{2,1,0:T(8,128)}, f32[7,512,128]{2,1,0:T(8,128)}, u32[]{:S(2)}, u32[]{:S(2)}) collective-permute-start(f32[7,512,128]{2,1,0:T(8,128)} %constant_dynamic-update-slice_fusion.11), channel_id=1, source_target_pairs={{0,1},{1,0},{2,3},{3,2},{4,5},{5,4},{6,7},{7,6},{8,9},{9,8},{10,11... | collective-permute-start | bytes 5505032 | tf_op jit(solution)/shard_map/ppermute | solution.py:132
  79.0 31.9 %shard_map.88.acc_ref = f32[6,192,128]{2,1,0:T(8,128)} custom-call(s32[12]{0:T(128)} %and_select_fusion.1.trips_ref, f32[1152]{0:T(1024)} %reshape.320.rows_ref, f32[7,256,128]{2,1,0:T(8,128)} %copy-done.1, f32[6,192,128]{2,1,0:T(8,128)} %shard_map.87.acc_ref), custom_call_target="tpu_custom_call", output_to_operand_aliasing={{}: (3, {})} | custom-call | flops 31457280000 | bytes 2097152 | tf_op jit(solution)/shard_map/pallas_call | solution.py:111
  110.9 60.2 %shard_map.89 = f32[6,192,128]{2,1,0:T(8,128)} custom-call(s32[12]{0:T(128)} %and_select_fusion.1.trips_ref, f32[1152]{0:T(1024)} %reshape.320.rows_ref, f32[7,512,128]{2,1,0:T(8,128)} %collective-permute-done.8.stars_ref, f32[6,192,128]{2,1,0:T(8,128)} %shard_map.88.acc_ref), custom_call_target="tpu_custom_call", output_to_operand_aliasing={{}: (3, {})} | custom-call | flops 62914560000 | bytes 3014656 | tf_op jit(solution)/shard_map/pallas_call | solution.py:111
  171.0 1.4 reduce_sum.9
  173.1 0.8 collective-permute-start.10
  173.8 1.1 collective-permute-start.11
  177.4 1.2 scatter_fusion.1
  178.6 0.8 copy.159
  179.7 1.2 scatter_fusion
  180.9 0.8 copy.158
  (95 shorter events, 12.9 us)
Async XLA Ops:
  0.6 8.8 %copy-start = (f32[1024]{0:T(1024)S(1)}, f32[1024]{0:T(1024)}, u32[]{:S(2)}) copy-start(f32[1024]{0:T(1024)} %param.11) | copy-start | bytes 12292
  3.6 13.7 %collective-permute-start.2 = (f32[7,8,128]{2,1,0:T(8,128)S(1)}, f32[7,8,128]{2,1,0:T(8,128)S(1)}, u32[]{:S(2)}, u32[]{:S(2)}) collective-permute-start(f32[7,8,128]{2,1,0:T(8,128)S(1)} %get-tuple-element.60), channel_id=1, source_target_pairs={{0,4},{4,0},{8,12},{12,8},{16,20},{20,16},{24,28},{28,24},{32,36},... | collective-permute-start | bytes 86024 | tf_op jit(solution)/shard_map/ppermute | solution.py:132
  3.8 13.5 %copy-start.7 = (f32[1024]{0:T(1024)S(1)}, f32[1024]{0:T(1024)}, u32[]{:S(2)}) copy-start(f32[1024]{0:T(1024)} %param.10) | copy-start | bytes 12292
  8.4 2.3 %collective-permute-start = (f32[7,192]{1,0:T(8,128)S(1)}, f32[7,192]{1,0:T(8,128)S(1)}, u32[]{:S(2)}, u32[]{:S(2)}) collective-permute-start(f32[7,192]{1,0:T(8,128)S(1)} %pad_maximum_fusion.4), channel_id=1, source_target_pairs={{0,1},{1,0},{2,3},{3,2},{4,5},{5,4},{6,7},{7,6},{8,9},{9,8},{10,11... | collective-permute-start | bytes 16136 | tf_op jit(solution)/shard_map/ppermute | solution.py:132
  10.8 3.1 %collective-permute-start.1 = (f32[7,384]{1,0:T(8,128)S(1)}, f32[7,384]{1,0:T(8,128)S(1)}, u32[]{:S(2)}, u32[]{:S(2)}) collective-permute-start(f32[7,384]{1,0:T(8,128)S(1)} %maximum_select_fusion.1), channel_id=1, source_target_pairs={{0,2},{1,3},{2,0},{3,1},{4,6},{5,7},{6,4},{7,5},{8,10},{9,11},{10,... | collective-permute-start | bytes 32264 | tf_op jit(solution)/shard_map/ppermute | solution.py:132
  17.3 3.3 %collective-permute-start.3 = (f32[7,16,128]{2,1,0:T(8,128)S(1)}, f32[7,16,128]{2,1,0:T(8,128)S(1)}, u32[]{:S(2)}, u32[]{:S(2)}) collective-permute-start(f32[7,16,128]{2,1,0:T(8,128)S(1)} %pad_maximum_fusion.2), channel_id=1, source_target_pairs={{0,8},{4,12},{8,0},{12,4},{16,24},{20,28},{24,16},{28,20},{32,40},... | collective-permute-start | bytes 172040 | tf_op jit(solution)/shard_map/ppermute | solution.py:132
  20.6 5.9 %collective-permute-start.4 = (f32[7,32,128]{2,1,0:T(8,128)S(1)}, f32[7,32,128]{2,1,0:T(8,128)S(1)}, u32[]{:S(2)}, u32[]{:S(2)}) collective-permute-start(f32[7,32,128]{2,1,0:T(8,128)S(1)} %pad_maximum_fusion.1), channel_id=1, source_target_pairs={{0,16},{4,20},{8,24},{12,28},{16,0},{20,4},{24,8},{28,12},{32,48},... | collective-permute-start | bytes 344072 | tf_op jit(solution)/shard_map/ppermute | solution.py:132
  26.5 2.2 %copy-start.4 = (f32[7,64,128]{2,1,0:T(8,128)}, f32[7,64,128]{2,1,0:T(8,128)S(1)}, u32[]{:S(2)}) copy-start(f32[7,64,128]{2,1,0:T(8,128)S(1)} %pad_maximum_fusion.stars_ref) | copy-start | bytes 688132
  26.5 13.7 %collective-permute-start.5 = (f32[7,64,128]{2,1,0:T(8,128)S(1)}, f32[7,64,128]{2,1,0:T(8,128)S(1)}, u32[]{:S(2)}, u32[]{:S(2)}) collective-permute-start(f32[7,64,128]{2,1,0:T(8,128)S(1)} %pad_maximum_fusion.stars_ref), channel_id=1, source_target_pairs={{0,32},{4,36},{8,40},{12,44},{16,48},{20,52},{24,56},{28,60},{32,0... | collective-permute-start | bytes 688136 | tf_op jit(solution)/shard_map/ppermute | solution.py:132
  40.2 3.0 %copy-start.3 = (f32[7,64,128]{2,1,0:T(8,128)}, f32[7,64,128]{2,1,0:T(8,128)S(1)}, u32[]{:S(2)}) copy-start(f32[7,64,128]{2,1,0:T(8,128)S(1)} %collective-permute-done.5.stars_ref) | copy-start | bytes 688132
  41.0 13.1 %collective-permute-start.6 = (f32[7,128,128]{2,1,0:T(8,128)S(1)}, f32[7,128,128]{2,1,0:T(8,128)S(1)}, u32[]{:S(2)}, u32[]{:S(2)}) collective-permute-start(f32[7,128,128]{2,1,0:T(8,128)S(1)} %get-tuple-element.45), channel_id=1, source_target_pairs={{0,64},{4,68},{8,72},{12,76},{16,80},{20,84},{24,88},{28,92},{32,9... | collective-permute-start | bytes 1376264 | tf_op jit(solution)/shard_map/ppermute | solution.py:132
  54.1 2.4 %copy-start.2 = (f32[7,128,128]{2,1,0:T(8,128)}, f32[7,128,128]{2,1,0:T(8,128)S(1)}, u32[]{:S(2)}) copy-start(f32[7,128,128]{2,1,0:T(8,128)S(1)} %collective-permute-done.6.stars_ref) | copy-start | bytes 1376260
  55.0 19.3 %collective-permute-start.7 = (f32[7,256,128]{2,1,0:T(8,128)S(1)}, f32[7,256,128]{2,1,0:T(8,128)S(1)}, u32[]{:S(2)}, u32[]{:S(2)}) collective-permute-start(f32[7,256,128]{2,1,0:T(8,128)S(1)} %get-tuple-element.41), channel_id=1, source_target_pairs={{0,2},{1,3},{2,0},{3,1},{4,6},{5,7},{6,4},{7,5},{8,10},{9,11},{10,... | collective-permute-start | bytes 2752520 | tf_op jit(solution)/shard_map/ppermute | solution.py:132
  74.3 4.7 %copy-start.1 = (f32[7,256,128]{2,1,0:T(8,128)}, f32[7,256,128]{2,1,0:T(8,128)S(1)}, u32[]{:S(2)}) copy-start(f32[7,256,128]{2,1,0:T(8,128)S(1)} %collective-permute-done.7.stars_ref) | copy-start | bytes 2752516
  75.3 35.5 %collective-permute-start.8 = (f32[7,512,128]{2,1,0:T(8,128)}, f32[7,512,128]{2,1,0:T(8,128)}, u32[]{:S(2)}, u32[]{:S(2)}) collective-permute-start(f32[7,512,128]{2,1,0:T(8,128)} %constant_dynamic-update-slice_fusion.11), channel_id=1, source_target_pairs={{0,1},{1,0},{2,3},{3,2},{4,5},{5,4},{6,7},{7,6},{8,9},{9,8},{10,11... | collective-permute-start | bytes 5505032 | tf_op jit(solution)/shard_map/ppermute | solution.py:132
  171.0 4.0 %copy-start.8 = (s32[3,1]{0,1:T(1,128)S(1)}, s32[3,1]{0,1:T(1,128)}, u32[]{:S(2)}) copy-start(s32[3,1]{0,1:T(1,128)} %param.13) | copy-start | bytes 40
  171.0 4.0 %copy-start.5 = (f32[6,1024]{1,0:T(8,128)S(1)}, f32[6,1024]{1,0:T(8,128)}, u32[]{:S(2)}) copy-start(f32[6,1024]{1,0:T(8,128)} %param.9) | copy-start | bytes 73732
  171.0 4.3 %copy-start.6 = (f32[6,1024]{1,0:T(8,128)S(1)}, f32[6,1024]{1,0:T(8,128)}, u32[]{:S(2)}) copy-start(f32[6,1024]{1,0:T(8,128)} %param.8) | copy-start | bytes 73732
  173.1 4.1 %collective-permute-start.10 = (f32[6,192]{1,0:T(8,128)S(1)}, f32[6,192]{1,0:T(8,128)S(1)}, u32[]{:S(2)}, u32[]{:S(2)}) collective-permute-start(f32[6,192]{1,0:T(8,128)S(1)} %bitcast.63), channel_id=1, source_target_pairs={{0,2},{1,3},{2,0},{3,1},{4,6},{5,7},{6,4},{7,5},{8,10},{9,11},{10,... | collective-permute-start | bytes 13832 | tf_op jit(solution)/shard_map/ppermute | solution.py:132
  173.8 3.4 %collective-permute-start.11 = (f32[6,192]{1,0:T(8,128)S(1)}, f32[6,192]{1,0:T(8,128)S(1)}, u32[]{:S(2)}, u32[]{:S(2)}) collective-permute-start(f32[6,192]{1,0:T(8,128)S(1)} %bitcast.64), channel_id=1, source_target_pairs={{0,3},{1,2},{2,1},{3,0},{4,7},{5,6},{6,5},{7,4},{8,11},{9,10},{10,... | collective-permute-start | bytes 13832 | tf_op jit(solution)/shard_map/ppermute | solution.py:132
  175.0 2.2 %collective-permute-start.9 = (f32[6,192]{1,0:T(8,128)S(1)}, f32[6,192]{1,0:T(8,128)S(1)}, u32[]{:S(2)}, u32[]{:S(2)}) collective-permute-start(f32[6,192]{1,0:T(8,128)S(1)} %bitcast.65), channel_id=1, source_target_pairs={{0,1},{1,0},{2,3},{3,2},{4,5},{5,4},{6,7},{7,6},{8,9},{9,8},{10,11... | collective-permute-start | bytes 13832 | tf_op jit(solution)/shard_map/ppermute | solution.py:132
